TPU v7x, 512 devices: a whole 4x4x16 slice. The times are simulated.
512 devices in a mesh: band: 32 (over x, z_lo), grid: 16 (over z_hi, y, core).
Axes of the slice: x: 4, y: 4, z: 16 (z_hi: 2, z_lo: 8; z = z_hi * 8 + z_lo), core: 2. Of those that a mesh axis runs over, the one named last changes fastest.
Arguments:
- trial_bands: float32 [64, 160, 32, 128], P('band', 'grid'), may hold values from -6 to 6
- potential: float32 [160, 32, 128], P('grid'), may hold values from -2 to 0
Outputs:
- filtered: float32 [64, 160, 32, 128], P('band', 'grid')
- projected: float32 [64, 64], P('band')
- residual_norms: float32 [64], P('band')
All inputs are finite; a program needn't handle non-finite values.
Results may differ from a plain program's by a relative error of at most 0.00016.
Values sent between devices are 32-bit elements; how exact they have to be, the bound alone decides.
No kernel may reach another device: no remote copies, remote signals or barrier semaphores. Data moves between devices by JAX's collectives and lax.ppermute only.
A program may use at most 64 MiB of HBM per device.

v0:
```python
import jax
import jax.numpy as jnp
from jax import lax
from jax.sharding import PartitionSpec as P

CENTER = 4.25
HALF_WIDTH = 3.75
LOWEST = -2.0
SIGMA_ONE = HALF_WIDTH / (LOWEST - CENTER)
FOUR_THIRDS = 4.0 / 3.0
TWELFTH = 1.0 / 12.0
filter_degree = 4


def padded_2(cells, sides, width):
    for axis, dim in sides:
        count = lax.axis_size(axis)
        head = lax.slice_in_dim(cells, 0, width, axis=dim)
        tail = lax.slice_in_dim(cells, cells.shape[dim] - width, cells.shape[dim], axis=dim)
        cells = jnp.concatenate(
            [
                lax.ppermute(tail, axis, [(i, (i + 1) % count) for i in range(count)]),
                cells,
                lax.ppermute(head, axis, [((i + 1) % count, i) for i in range(count)]),
            ],
            axis=dim,
        )
    return cells


def operate(field_in, potential):
    padded = padded_2(field_in, (("grid", 1),), 2)
    plane_count = field_in.shape[1]
    near_sum = padded[:, 1 : 1 + plane_count] + padded[:, 3 : 3 + plane_count]
    near_sum = near_sum + jnp.roll(field_in, 1, 2) + jnp.roll(field_in, -1, 2)
    near_sum = near_sum + jnp.roll(field_in, 1, 3) + jnp.roll(field_in, -1, 3)
    far_sum = padded[:, 0:plane_count] + padded[:, 4 : 4 + plane_count]
    far_sum = far_sum + jnp.roll(field_in, 2, 2) + jnp.roll(field_in, -2, 2)
    far_sum = far_sum + jnp.roll(field_in, 2, 3) + jnp.roll(field_in, -2, 3)
    kinetic = 0.5 * (7.5 * field_in - FOUR_THIRDS * near_sum + TWELFTH * far_sum)
    return kinetic + potential * field_in


def on_device(trial_bands, potential):
    sigma_now = SIGMA_ONE
    previous = trial_bands
    current = (operate(trial_bands, potential) - CENTER * trial_bands) * (SIGMA_ONE / HALF_WIDTH)
    for repeat_index in range(filter_degree - 1):
        sigma_next = 1.0 / (2.0 / SIGMA_ONE - sigma_now)
        following = (operate(current, potential) - CENTER * current) * (
            2.0 * sigma_next / HALF_WIDTH
        ) - sigma_now * sigma_next * previous
        previous, current, sigma_now = (current, following, sigma_next)
    applied = operate(current, potential)
    band_count = current.shape[0]
    band_devices = lax.axis_size("band")
    total_bands = band_count * band_devices
    cell_count = current.shape[1] * current.shape[2] * current.shape[3]
    cell_total = cell_count * lax.axis_size("grid")
    inverse_cells = 1.0 / cell_total
    first_band = lax.axis_index("band") * band_count
    both = jnp.stack(
        [current.reshape(band_count, cell_count), applied.reshape(band_count, cell_count)]
    ).reshape(2, band_count, band_devices, cell_count // band_devices)
    moved = lax.all_to_all(both, "band", 2, 1, tiled=True)
    bands_here = moved[0].reshape(total_bands, -1)
    image_here = moved[1].reshape(total_bands, -1)
    margin_part = jnp.dot(
        bands_here,
        bands_here.T,
        precision=lax.Precision.HIGHEST,
        preferred_element_type=jnp.float32,
    )
    image_part = jnp.dot(
        image_here,
        bands_here.T,
        precision=lax.Precision.HIGHEST,
        preferred_element_type=jnp.float32,
    )
    norm_part = jnp.sum(image_here * image_here, axis=1)
    packed = jnp.concatenate([margin_part.reshape(-1), image_part.reshape(-1), norm_part])
    packed = lax.psum(packed, ("band", "grid")) * inverse_cells
    square = total_bands * total_bands
    margin = packed[:square].reshape(total_bands, total_bands)
    subspace = packed[square : 2 * square].reshape(total_bands, total_bands)
    image_norms = packed[2 * square :]
    factor = jnp.linalg.cholesky(margin)
    coefficients = lax.linalg.triangular_solve(factor, subspace.T, left_side=True, lower=True)
    projected = lax.linalg.triangular_solve(factor, coefficients.T, left_side=True, lower=True)
    residual_norms = image_norms - jnp.sum(coefficients * coefficients, axis=0)
    projected_rows = lax.dynamic_slice_in_dim(projected, first_band, band_count, 0)
    residual_rows = lax.dynamic_slice_in_dim(residual_norms, first_band, band_count, 0)
    return (current, projected_rows, residual_rows)


def solution(mesh):
    in_specs = (P("band", "grid", None, None), P("grid", None, None))
    out_specs = (P("band", "grid", None, None), P("band", None), P("band"))
    return jax.shard_map(
        on_device, mesh=mesh, in_specs=in_specs, out_specs=out_specs, check_vma=False
    )
```

profile of v0, /device:TPU:1, one launch (start us, length us, event | category | flops | bytes accessed | tf_op | source)
XLA Modules:
  0.0 275.6 jit_solution(5035472801133282586)
XLA Ops:
  0.6 0.9 fusion.146
  1.5 4.6 %collective-permute-start = (f32[2,2,32,128]{3,2,1,0:T(8,128)S(1)}, f32[2,2,32,128]{3,2,1,0:T(8,128)S(1)}, u32[]{:S(2)}, u32[]{:S(2)}) collective-permute-start(f32[2,2,32,128]{3,2,1,0:T(8,128)S(1)} %get-tuple-element.91), channel_id=1, source_target_pairs={{0,1},{1,2},{2,3},{3,4},{4,5},{5,6},{6,7},{7,8},{8,9},{9,10},{10,1... | collective-permute-start | bytes 196616 | tf_op jit(solution)/shard_map/ppermute | solution.py:22
  6.1 6.2 %collective-permute-start.1 = (f32[2,2,32,128]{3,2,1,0:T(8,128)S(1)}, f32[2,2,32,128]{3,2,1,0:T(8,128)S(1)}, u32[]{:S(2)}, u32[]{:S(2)}) collective-permute-start(f32[2,2,32,128]{3,2,1,0:T(8,128)S(1)} %get-tuple-element.92), channel_id=1, source_target_pairs={{1,0},{2,1},{3,2},{4,3},{5,4},{6,5},{7,6},{8,7},{9,8},{10,9},{11,1... | collective-permute-start | bytes 196616 | tf_op jit(solution)/shard_map/ppermute | solution.py:24
  12.4 1.2 fusion.150
  13.8 0.2 fusion.145
  14.3 0.7 copy-done.2
  15.2 0.7 broadcast_multiply_fusion
  16.0 0.2 fusion.134
  16.4 0.2 fusion.138
  16.7 1.9 collective-permute-start.2
  18.6 14.5 %collective-permute-start.3 = (f32[2,2,32,128]{3,2,1,0:T(8,128)S(1)}, f32[2,2,32,128]{3,2,1,0:T(8,128)S(1)}, u32[]{:S(2)}, u32[]{:S(2)}) collective-permute-start(f32[2,2,32,128]{3,2,1,0:T(8,128)S(1)} %get-tuple-element.80), channel_id=1, source_target_pairs={{1,0},{2,1},{3,2},{4,3},{5,4},{6,5},{7,6},{8,7},{9,8},{10,9},{11,1... | collective-permute-start | bytes 196616 | tf_op jit(solution)/shard_map/ppermute | solution.py:24
  33.1 0.8 collective-permute-done.3
  34.0 0.7 fusion.55
  35.5 1.9 collective-permute-start.4
  37.4 15.5 %collective-permute-start.5 = (f32[2,2,32,128]{3,2,1,0:T(8,128)S(1)}, f32[2,2,32,128]{3,2,1,0:T(8,128)S(1)}, u32[]{:S(2)}, u32[]{:S(2)}) collective-permute-start(f32[2,2,32,128]{3,2,1,0:T(8,128)S(1)} %get-tuple-element.62), channel_id=1, source_target_pairs={{1,0},{2,1},{3,2},{4,3},{5,4},{6,5},{7,6},{8,7},{9,8},{10,9},{11,1... | collective-permute-start | bytes 196616 | tf_op jit(solution)/shard_map/ppermute | solution.py:24
  52.9 0.8 collective-permute-done.5
  53.8 0.6 fusion.40
  55.2 1.9 collective-permute-start.6
  57.2 15.5 %collective-permute-start.7 = (f32[2,2,32,128]{3,2,1,0:T(8,128)S(1)}, f32[2,2,32,128]{3,2,1,0:T(8,128)S(1)}, u32[]{:S(2)}, u32[]{:S(2)}) collective-permute-start(f32[2,2,32,128]{3,2,1,0:T(8,128)S(1)} %get-tuple-element.44), channel_id=1, source_target_pairs={{1,0},{2,1},{3,2},{4,3},{5,4},{6,5},{7,6},{8,7},{9,8},{10,9},{11,1... | collective-permute-start | bytes 196616 | tf_op jit(solution)/shard_map/ppermute | solution.py:24
  72.7 0.8 collective-permute-done.7
  73.6 0.6 fusion.25
  74.8 0.9 fusion.111
  75.7 0.9 fusion.112
  76.6 0.7 fusion.114
  77.3 1.9 collective-permute-start.8
  79.2 15.5 %collective-permute-start.9 = (f32[2,2,32,128]{3,2,1,0:T(8,128)}, f32[2,2,32,128]{3,2,1,0:T(8,128)}, u32[]{:S(2)}, u32[]{:S(2)}) collective-permute-start(f32[2,2,32,128]{3,2,1,0:T(8,128)} %get-tuple-element.26), channel_id=1, source_target_pairs={{1,0},{2,1},{3,2},{4,3},{5,4},{6,5},{7,6},{8,7},{9,8},{10,9},{11,1... | collective-permute-start | bytes 196616 | tf_op jit(solution)/shard_map/ppermute | solution.py:24
  94.7 0.6 fusion.113
  95.4 0.8 stack.7
  96.2 0.7 copy-done.4
  96.9 2.5 fusion.10
  99.4 1.1 stack.8
  100.5 1.4 copy.10
  101.9 10.4 %all-to-all-start = ((f32[2,2,32,1280]{3,1,0,2:T(2,128)}), f32[2,2,32,1280]{3,1,0,2:T(2,128)S(1)}, u32[]{:S(2)}, u32[]{:S(2)}) async-start(f32[2,2,32,1280]{3,1,0,2:T(2,128)} %copy.10), calls=%async_computation | async-start | bytes 1310720 | tf_op jit(solution)/shard_map/all_to_all | solution.py:65
  112.3 22.4 %all-to-all-done = f32[2,2,32,1280]{3,1,0,2:T(2,128)S(1)} async-done(((f32[2,2,32,1280]{3,1,0,2:T(2,128)}), f32[2,2,32,1280]{3,1,0,2:T(2,128)S(1)}, u32[]{:S(2)}, u32[]{:S(2)}) %all-to-all-start) | async-done | bytes 655392 | tf_op jit(solution)/shard_map/all_to_all | solution.py:65
  134.7 0.3 fusion.105
  135.0 0.2 reshape_squeeze.6
  135.2 0.2 reshape_squeeze.7
  135.4 0.4 fusion.152
  135.8 0.4 fusion.153
  136.5 125.1 %psum.7 = f32[8256]{0:T(1024)S(1)} all-reduce(f32[8256]{0:T(1024)S(1)} %pad_maximum_fusion.9), channel_id=1, replica_groups=mesh['band'=32,'grid'=16] {'band','grid'}, use_global_device_ids=true, to_apply=%region_1.2 | all-reduce | flops 8256 | bytes 66048 | tf_op jit(solution)/shard_map/psum | solution.py:82
  261.8 5.8 %cholesky.18 = f32[64,64]{1,0:T(8,128)S(1)} custom-call(f32[64,64]{1,0:T(8,128)S(1)} %fusion.103), custom_call_target="Cholesky" | custom-call | tf_op jit(solution)/shard_map/jit(cholesky)/cholesky | solution.py:87
  267.7 0.6 compare_reduce_fusion
  268.3 0.7 fusion.96
  269.0 4.9 %custom-call.8 = f32[1,64,64]{1,2,0:T(8,128)S(1)} custom-call(f32[1,64,64]{2,1,0:T(8,128)S(1)} %fusion.96), custom_call_target="InvertDiagBlocksLowerTriangular" | custom-call | tf_op jit(solution)/shard_map/triangular_solve/custom-call.0 | solution.py:89
  273.9 0.3 multiply_reduce_fusion.1
  274.2 0.2 fusion.97
  274.4 0.6 dynamic_slice.7
  275.0 0.6 constant_dynamic-slice_fusion
  (70 shorter events, 3.9 us)
Async XLA Ops:
  1.5 13.5 %collective-permute-start = (f32[2,2,32,128]{3,2,1,0:T(8,128)S(1)}, f32[2,2,32,128]{3,2,1,0:T(8,128)S(1)}, u32[]{:S(2)}, u32[]{:S(2)}) collective-permute-start(f32[2,2,32,128]{3,2,1,0:T(8,128)S(1)} %get-tuple-element.91), channel_id=1, source_target_pairs={{0,1},{1,2},{2,3},{3,4},{4,5},{5,6},{6,7},{7,8},{8,9},{9,10},{10,1... | collective-permute-start | bytes 196616 | tf_op jit(solution)/shard_map/ppermute | solution.py:22
  6.1 7.5 %copy-start.1 = (f32[2,10,32,128]{3,2,1,0:T(8,128)S(1)}, f32[2,10,32,128]{3,2,1,0:T(8,128)}, u32[]{:S(2)}) copy-start(f32[2,10,32,128]{3,2,1,0:T(8,128)} %param.4) | copy-start | bytes 983044
  6.1 9.0 %collective-permute-start.1 = (f32[2,2,32,128]{3,2,1,0:T(8,128)S(1)}, f32[2,2,32,128]{3,2,1,0:T(8,128)S(1)}, u32[]{:S(2)}, u32[]{:S(2)}) collective-permute-start(f32[2,2,32,128]{3,2,1,0:T(8,128)S(1)} %get-tuple-element.92), channel_id=1, source_target_pairs={{1,0},{2,1},{3,2},{4,3},{5,4},{6,5},{7,6},{8,7},{9,8},{10,9},{11,1... | collective-permute-start | bytes 196616 | tf_op jit(solution)/shard_map/ppermute | solution.py:24
  14.1 0.9 copy-start.2
  16.7 16.4 %collective-permute-start.2 = (f32[2,2,32,128]{3,2,1,0:T(8,128)S(1)}, f32[2,2,32,128]{3,2,1,0:T(8,128)S(1)}, u32[]{:S(2)}, u32[]{:S(2)}) collective-permute-start(f32[2,2,32,128]{3,2,1,0:T(8,128)S(1)} %get-tuple-element.79), channel_id=1, source_target_pairs={{0,1},{1,2},{2,3},{3,4},{4,5},{5,6},{6,7},{7,8},{8,9},{9,10},{10,1... | collective-permute-start | bytes 196616 | tf_op jit(solution)/shard_map/ppermute | solution.py:22
  18.6 15.4 %collective-permute-start.3 = (f32[2,2,32,128]{3,2,1,0:T(8,128)S(1)}, f32[2,2,32,128]{3,2,1,0:T(8,128)S(1)}, u32[]{:S(2)}, u32[]{:S(2)}) collective-permute-start(f32[2,2,32,128]{3,2,1,0:T(8,128)S(1)} %get-tuple-element.80), channel_id=1, source_target_pairs={{1,0},{2,1},{3,2},{4,3},{5,4},{6,5},{7,6},{8,7},{9,8},{10,9},{11,1... | collective-permute-start | bytes 196616 | tf_op jit(solution)/shard_map/ppermute | solution.py:24
  35.5 17.4 %collective-permute-start.4 = (f32[2,2,32,128]{3,2,1,0:T(8,128)S(1)}, f32[2,2,32,128]{3,2,1,0:T(8,128)S(1)}, u32[]{:S(2)}, u32[]{:S(2)}) collective-permute-start(f32[2,2,32,128]{3,2,1,0:T(8,128)S(1)} %get-tuple-element.61), channel_id=1, source_target_pairs={{0,1},{1,2},{2,3},{3,4},{4,5},{5,6},{6,7},{7,8},{8,9},{9,10},{10,1... | collective-permute-start | bytes 196616 | tf_op jit(solution)/shard_map/ppermute | solution.py:22
  37.4 16.4 %collective-permute-start.5 = (f32[2,2,32,128]{3,2,1,0:T(8,128)S(1)}, f32[2,2,32,128]{3,2,1,0:T(8,128)S(1)}, u32[]{:S(2)}, u32[]{:S(2)}) collective-permute-start(f32[2,2,32,128]{3,2,1,0:T(8,128)S(1)} %get-tuple-element.62), channel_id=1, source_target_pairs={{1,0},{2,1},{3,2},{4,3},{5,4},{6,5},{7,6},{8,7},{9,8},{10,9},{11,1... | collective-permute-start | bytes 196616 | tf_op jit(solution)/shard_map/ppermute | solution.py:24
  55.2 17.5 %collective-permute-start.6 = (f32[2,2,32,128]{3,2,1,0:T(8,128)S(1)}, f32[2,2,32,128]{3,2,1,0:T(8,128)S(1)}, u32[]{:S(2)}, u32[]{:S(2)}) collective-permute-start(f32[2,2,32,128]{3,2,1,0:T(8,128)S(1)} %get-tuple-element.43), channel_id=1, source_target_pairs={{0,1},{1,2},{2,3},{3,4},{4,5},{5,6},{6,7},{7,8},{8,9},{9,10},{10,1... | collective-permute-start | bytes 196616 | tf_op jit(solution)/shard_map/ppermute | solution.py:22
  57.2 16.4 %collective-permute-start.7 = (f32[2,2,32,128]{3,2,1,0:T(8,128)S(1)}, f32[2,2,32,128]{3,2,1,0:T(8,128)S(1)}, u32[]{:S(2)}, u32[]{:S(2)}) collective-permute-start(f32[2,2,32,128]{3,2,1,0:T(8,128)S(1)} %get-tuple-element.44), channel_id=1, source_target_pairs={{1,0},{2,1},{3,2},{4,3},{5,4},{6,5},{7,6},{8,7},{9,8},{10,9},{11,1... | collective-permute-start | bytes 196616 | tf_op jit(solution)/shard_map/ppermute | solution.py:24
  74.2 21.9 %copy-start = (f32[2,10,32,128]{3,2,1,0:T(8,128)}, f32[2,10,32,128]{3,2,1,0:T(8,128)S(1)}, u32[]{:S(2)}) copy-start(f32[2,10,32,128]{3,2,1,0:T(8,128)S(1)} %fusion.25) | copy-start | bytes 983044
  77.3 18.9 %collective-permute-start.8 = (f32[2,2,32,128]{3,2,1,0:T(8,128)}, f32[2,2,32,128]{3,2,1,0:T(8,128)S(1)}, u32[]{:S(2)}, u32[]{:S(2)}) collective-permute-start(f32[2,2,32,128]{3,2,1,0:T(8,128)} %get-tuple-element.25), channel_id=1, source_target_pairs={{0,1},{1,2},{2,3},{3,4},{4,5},{5,6},{6,7},{7,8},{8,9},{9,10},{10,1... | collective-permute-start | bytes 196616 | tf_op jit(solution)/shard_map/ppermute | solution.py:22
  79.2 16.9 %collective-permute-start.9 = (f32[2,2,32,128]{3,2,1,0:T(8,128)}, f32[2,2,32,128]{3,2,1,0:T(8,128)}, u32[]{:S(2)}, u32[]{:S(2)}) collective-permute-start(f32[2,2,32,128]{3,2,1,0:T(8,128)} %get-tuple-element.26), channel_id=1, source_target_pairs={{1,0},{2,1},{3,2},{4,3},{5,4},{6,5},{7,6},{8,7},{9,8},{10,9},{11,1... | collective-permute-start | bytes 196616 | tf_op jit(solution)/shard_map/ppermute | solution.py:24
  96.1 0.7 copy-start.4
  96.1 0.7 copy-start.5
  99.4 1.1 copy-start.3
  101.9 32.8 %all-to-all-start = ((f32[2,2,32,1280]{3,1,0,2:T(2,128)}), f32[2,2,32,1280]{3,1,0,2:T(2,128)S(1)}, u32[]{:S(2)}, u32[]{:S(2)}) async-start(f32[2,2,32,1280]{3,1,0,2:T(2,128)} %copy.10), calls=%async_computation | async-start | bytes 1310720 | tf_op jit(solution)/shard_map/all_to_all | solution.py:65
where the time goes:
time: 276 us
  blocking collectives  125 us (45%)
  starting transfers between devices  89.9 us (33%)
  waiting for transfers between devices  25 us (9%)
  other arithmetic  17.6 us (6%)
  local copies, waits for them, and re-layouts  15.7 us (6%)
    psum x1, blocking collectives, on_device(): packed = lax.psum(packed, ('band', 'grid')) * inverse_cells  125 us
    ppermute x5, starting transfers between devices, padded_2(): lax.ppermute(head, axis, [((i + 1) % count, i) for i in range(count)])  67.2 us
    all_to_all x1, waiting for transfers between devices, on_device(): moved = lax.all_to_all(both, 'band', 2, 1, tiled=True)  22.4 us
    ppermute x5, starting transfers between devices, padded_2(): lax.ppermute(tail, axis, [(i, (i + 1) % count) for i in range(count)])  12.3 us
    all_to_all x1, starting transfers between devices, on_device(): moved = lax.all_to_all(both, 'band', 2, 1, tiled=True)  10.4 us
    another operation x3, other arithmetic, on_device(): factor = jnp.linalg.cholesky(margin)  6.52 us
    another operation x2, other arithmetic, on_device(): lax.linalg.triangular_solve(factor, coefficients.T, left_side=True, lower...  5.55 us
  transfers between devices with their start and end apart: 11, of which 4 were waited for; matrix products, arithmetic and copies ran while one was open for 1% of the time, Pallas kernels for 0%

commit v1 on v0

--- a/solution.py
+++ b/solution.py
@@ -79,7 +79,7 @@
     )
     norm_part = jnp.sum(image_here * image_here, axis=1)
     packed = jnp.concatenate([margin_part.reshape(-1), image_part.reshape(-1), norm_part])
-    packed = lax.psum(packed, ("band", "grid")) * inverse_cells
+    packed = lax.psum(lax.psum(packed, "band"), "grid") * inverse_cells
     square = total_bands * total_bands
     margin = packed[:square].reshape(total_bands, total_bands)
     subspace = packed[square : 2 * square].reshape(total_bands, total_bands)

time: 276 us -> 513 us (1.86); the launches traced: 276 us -> 503 us
  blocking collectives: 125 us -> 352 us
    psum x1 -> x2, blocking collectives: 125 us -> 352 us  [on_device(): packed = lax.psum(lax.psum(packed, 'band'), 'grid') * inverse_cells]
where the time goes in v1:
time: 513 us; the launch traced here: 503 us
  blocking collectives  352 us (69%)
  starting transfers between devices  89.9 us (18%)
  waiting for transfers between devices  25 us (5%)
  other arithmetic  17.6 us (3%)
  local copies, waits for them, and re-layouts  15.7 us (3%)
    psum x2, blocking collectives, on_device(): packed = lax.psum(lax.psum(packed, 'band'), 'grid') * inverse_cells  352 us
    ppermute x5, starting transfers between devices, padded_2(): lax.ppermute(head, axis, [((i + 1) % count, i) for i in range(count)])  67.2 us
    all_to_all x1, waiting for transfers between devices, on_device(): moved = lax.all_to_all(both, 'band', 2, 1, tiled=True)  22.4 us
    ppermute x5, starting transfers between devices, padded_2(): lax.ppermute(tail, axis, [(i, (i + 1) % count) for i in range(count)])  12.3 us
    all_to_all x1, starting transfers between devices, on_device(): moved = lax.all_to_all(both, 'band', 2, 1, tiled=True)  10.4 us
  transfers between devices with their start and end apart: 11, of which 4 were waited for; matrix products, arithmetic and copies ran while one was open for 1% of the time, Pallas kernels for 0%

profile of v1, /device:TPU:1, one launch (start us, length us, event | category | flops | bytes accessed | tf_op | source)
XLA Modules:
  0.0 503.0 jit_solution(14452085747746712297)
XLA Ops:
  0.6 0.9 fusion.146
  1.5 4.6 collective-permute-start
  6.1 6.2 %collective-permute-start.1 = (f32[2,2,32,128]{3,2,1,0:T(8,128)S(1)}, f32[2,2,32,128]{3,2,1,0:T(8,128)S(1)}, u32[]{:S(2)}, u32[]{:S(2)}) collective-permute-start(f32[2,2,32,128]{3,2,1,0:T(8,128)S(1)} %get-tuple-element.92), channel_id=1, source_target_pairs={{1,0},{2,1},{3,2},{4,3},{5,4},{6,5},{7,6},{8,7},{9,8},{10,9},{11,1... | collective-permute-start | bytes 196616 | tf_op jit(solution)/shard_map/ppermute | solution.py:24
  12.4 1.2 fusion.150
  13.8 0.2 fusion.145
  14.3 0.7 copy-done.2
  15.2 0.7 broadcast_multiply_fusion
  16.0 0.2 fusion.134
  16.7 1.9 collective-permute-start.2
  18.6 14.5 %collective-permute-start.3 = (f32[2,2,32,128]{3,2,1,0:T(8,128)S(1)}, f32[2,2,32,128]{3,2,1,0:T(8,128)S(1)}, u32[]{:S(2)}, u32[]{:S(2)}) collective-permute-start(f32[2,2,32,128]{3,2,1,0:T(8,128)S(1)} %get-tuple-element.80), channel_id=1, source_target_pairs={{1,0},{2,1},{3,2},{4,3},{5,4},{6,5},{7,6},{8,7},{9,8},{10,9},{11,1... | collective-permute-start | bytes 196616 | tf_op jit(solution)/shard_map/ppermute | solution.py:24
  33.1 0.8 collective-permute-done.3
  34.0 0.7 fusion.55
  35.5 1.9 collective-permute-start.4
  37.4 15.5 %collective-permute-start.5 = (f32[2,2,32,128]{3,2,1,0:T(8,128)S(1)}, f32[2,2,32,128]{3,2,1,0:T(8,128)S(1)}, u32[]{:S(2)}, u32[]{:S(2)}) collective-permute-start(f32[2,2,32,128]{3,2,1,0:T(8,128)S(1)} %get-tuple-element.62), channel_id=1, source_target_pairs={{1,0},{2,1},{3,2},{4,3},{5,4},{6,5},{7,6},{8,7},{9,8},{10,9},{11,1... | collective-permute-start | bytes 196616 | tf_op jit(solution)/shard_map/ppermute | solution.py:24
  52.9 0.8 collective-permute-done.5
  53.8 0.6 fusion.40
  55.2 1.9 collective-permute-start.6
  57.2 15.5 %collective-permute-start.7 = (f32[2,2,32,128]{3,2,1,0:T(8,128)S(1)}, f32[2,2,32,128]{3,2,1,0:T(8,128)S(1)}, u32[]{:S(2)}, u32[]{:S(2)}) collective-permute-start(f32[2,2,32,128]{3,2,1,0:T(8,128)S(1)} %get-tuple-element.44), channel_id=1, source_target_pairs={{1,0},{2,1},{3,2},{4,3},{5,4},{6,5},{7,6},{8,7},{9,8},{10,9},{11,1... | collective-permute-start | bytes 196616 | tf_op jit(solution)/shard_map/ppermute | solution.py:24
  72.7 0.8 collective-permute-done.7
  73.6 0.6 fusion.25
  74.8 0.9 fusion.111
  75.7 0.9 fusion.112
  76.7 0.7 fusion.114
  77.3 1.9 collective-permute-start.8
  79.3 15.5 %collective-permute-start.9 = (f32[2,2,32,128]{3,2,1,0:T(8,128)}, f32[2,2,32,128]{3,2,1,0:T(8,128)}, u32[]{:S(2)}, u32[]{:S(2)}) collective-permute-start(f32[2,2,32,128]{3,2,1,0:T(8,128)} %get-tuple-element.26), channel_id=1, source_target_pairs={{1,0},{2,1},{3,2},{4,3},{5,4},{6,5},{7,6},{8,7},{9,8},{10,9},{11,1... | collective-permute-start | bytes 196616 | tf_op jit(solution)/shard_map/ppermute | solution.py:24
  94.8 0.6 fusion.113
  95.4 0.8 stack.7
  96.2 0.7 copy-done.4
  96.9 2.5 fusion.10
  99.5 1.1 stack.8
  100.6 1.4 copy.10
  102.0 10.4 %all-to-all-start = ((f32[2,2,32,1280]{3,1,0,2:T(2,128)}), f32[2,2,32,1280]{3,1,0,2:T(2,128)S(1)}, u32[]{:S(2)}, u32[]{:S(2)}) async-start(f32[2,2,32,1280]{3,1,0,2:T(2,128)} %copy.10), calls=%async_computation | async-start | bytes 1310720 | tf_op jit(solution)/shard_map/all_to_all | solution.py:65
  112.3 22.4 %all-to-all-done = f32[2,2,32,1280]{3,1,0,2:T(2,128)S(1)} async-done(((f32[2,2,32,1280]{3,1,0,2:T(2,128)}), f32[2,2,32,1280]{3,1,0,2:T(2,128)S(1)}, u32[]{:S(2)}, u32[]{:S(2)}) %all-to-all-start) | async-done | bytes 655392 | tf_op jit(solution)/shard_map/all_to_all | solution.py:65
  134.8 0.3 fusion.105
  135.0 0.2 reshape_squeeze.6
  135.3 0.2 reshape_squeeze.7
  135.5 0.4 fusion.152
  135.9 0.4 fusion.153
  136.6 200.3 %psum.14 = f32[8256]{0:T(1024)S(1)} all-reduce(f32[8256]{0:T(1024)S(1)} %pad_maximum_fusion.9), channel_id=1, replica_groups=mesh['band'=32,'grid'=16] {'band'}, use_global_device_ids=true, to_apply=%region_1.2 | all-reduce | flops 8256 | bytes 66048 | tf_op jit(solution)/shard_map/psum | solution.py:82
  336.9 152.1 %psum.15 = f32[8256]{0:T(1024)S(1)} all-reduce(f32[8256]{0:T(1024)S(1)} %psum.14), channel_id=1, replica_groups=mesh['band'=32,'grid'=16] {'grid'}, use_global_device_ids=true, to_apply=%region_2.3 | all-reduce | flops 8256 | bytes 66048 | tf_op jit(solution)/shard_map/psum | solution.py:82
  489.2 5.8 %cholesky.18 = f32[64,64]{1,0:T(8,128)S(1)} custom-call(f32[64,64]{1,0:T(8,128)S(1)} %fusion.103), custom_call_target="Cholesky" | custom-call | tf_op jit(solution)/shard_map/jit(cholesky)/cholesky | solution.py:87
  495.1 0.6 compare_reduce_fusion
  495.7 0.7 fusion.96
  496.4 4.9 custom-call.8
  501.4 0.3 multiply_reduce_fusion.1
  501.6 0.2 fusion.97
  501.9 0.6 dynamic_slice.7
  502.5 0.6 constant_dynamic-slice_fusion
  (71 shorter events, 4.1 us)
Async XLA Ops:
  1.5 13.5 %collective-permute-start = (f32[2,2,32,128]{3,2,1,0:T(8,128)S(1)}, f32[2,2,32,128]{3,2,1,0:T(8,128)S(1)}, u32[]{:S(2)}, u32[]{:S(2)}) collective-permute-start(f32[2,2,32,128]{3,2,1,0:T(8,128)S(1)} %get-tuple-element.91), channel_id=1, source_target_pairs={{0,1},{1,2},{2,3},{3,4},{4,5},{5,6},{6,7},{7,8},{8,9},{9,10},{10,1... | collective-permute-start | bytes 196616 | tf_op jit(solution)/shard_map/ppermute | solution.py:22
  6.1 7.5 %copy-start.1 = (f32[2,10,32,128]{3,2,1,0:T(8,128)S(1)}, f32[2,10,32,128]{3,2,1,0:T(8,128)}, u32[]{:S(2)}) copy-start(f32[2,10,32,128]{3,2,1,0:T(8,128)} %param.4) | copy-start | bytes 983044
  6.1 9.0 %collective-permute-start.1 = (f32[2,2,32,128]{3,2,1,0:T(8,128)S(1)}, f32[2,2,32,128]{3,2,1,0:T(8,128)S(1)}, u32[]{:S(2)}, u32[]{:S(2)}) collective-permute-start(f32[2,2,32,128]{3,2,1,0:T(8,128)S(1)} %get-tuple-element.92), channel_id=1, source_target_pairs={{1,0},{2,1},{3,2},{4,3},{5,4},{6,5},{7,6},{8,7},{9,8},{10,9},{11,1... | collective-permute-start | bytes 196616 | tf_op jit(solution)/shard_map/ppermute | solution.py:24
  14.1 0.9 copy-start.2
  16.7 16.4 %collective-permute-start.2 = (f32[2,2,32,128]{3,2,1,0:T(8,128)S(1)}, f32[2,2,32,128]{3,2,1,0:T(8,128)S(1)}, u32[]{:S(2)}, u32[]{:S(2)}) collective-permute-start(f32[2,2,32,128]{3,2,1,0:T(8,128)S(1)} %get-tuple-element.79), channel_id=1, source_target_pairs={{0,1},{1,2},{2,3},{3,4},{4,5},{5,6},{6,7},{7,8},{8,9},{9,10},{10,1... | collective-permute-start | bytes 196616 | tf_op jit(solution)/shard_map/ppermute | solution.py:22
  18.6 15.4 %collective-permute-start.3 = (f32[2,2,32,128]{3,2,1,0:T(8,128)S(1)}, f32[2,2,32,128]{3,2,1,0:T(8,128)S(1)}, u32[]{:S(2)}, u32[]{:S(2)}) collective-permute-start(f32[2,2,32,128]{3,2,1,0:T(8,128)S(1)} %get-tuple-element.80), channel_id=1, source_target_pairs={{1,0},{2,1},{3,2},{4,3},{5,4},{6,5},{7,6},{8,7},{9,8},{10,9},{11,1... | collective-permute-start | bytes 196616 | tf_op jit(solution)/shard_map/ppermute | solution.py:24
  35.5 17.4 %collective-permute-start.4 = (f32[2,2,32,128]{3,2,1,0:T(8,128)S(1)}, f32[2,2,32,128]{3,2,1,0:T(8,128)S(1)}, u32[]{:S(2)}, u32[]{:S(2)}) collective-permute-start(f32[2,2,32,128]{3,2,1,0:T(8,128)S(1)} %get-tuple-element.61), channel_id=1, source_target_pairs={{0,1},{1,2},{2,3},{3,4},{4,5},{5,6},{6,7},{7,8},{8,9},{9,10},{10,1... | collective-permute-start | bytes 196616 | tf_op jit(solution)/shard_map/ppermute | solution.py:22
  37.4 16.4 %collective-permute-start.5 = (f32[2,2,32,128]{3,2,1,0:T(8,128)S(1)}, f32[2,2,32,128]{3,2,1,0:T(8,128)S(1)}, u32[]{:S(2)}, u32[]{:S(2)}) collective-permute-start(f32[2,2,32,128]{3,2,1,0:T(8,128)S(1)} %get-tuple-element.62), channel_id=1, source_target_pairs={{1,0},{2,1},{3,2},{4,3},{5,4},{6,5},{7,6},{8,7},{9,8},{10,9},{11,1... | collective-permute-start | bytes 196616 | tf_op jit(solution)/shard_map/ppermute | solution.py:24
  55.2 17.5 %collective-permute-start.6 = (f32[2,2,32,128]{3,2,1,0:T(8,128)S(1)}, f32[2,2,32,128]{3,2,1,0:T(8,128)S(1)}, u32[]{:S(2)}, u32[]{:S(2)}) collective-permute-start(f32[2,2,32,128]{3,2,1,0:T(8,128)S(1)} %get-tuple-element.43), channel_id=1, source_target_pairs={{0,1},{1,2},{2,3},{3,4},{4,5},{5,6},{6,7},{7,8},{8,9},{9,10},{10,1... | collective-permute-start | bytes 196616 | tf_op jit(solution)/shard_map/ppermute | solution.py:22
  57.2 16.4 %collective-permute-start.7 = (f32[2,2,32,128]{3,2,1,0:T(8,128)S(1)}, f32[2,2,32,128]{3,2,1,0:T(8,128)S(1)}, u32[]{:S(2)}, u32[]{:S(2)}) collective-permute-start(f32[2,2,32,128]{3,2,1,0:T(8,128)S(1)} %get-tuple-element.44), channel_id=1, source_target_pairs={{1,0},{2,1},{3,2},{4,3},{5,4},{6,5},{7,6},{8,7},{9,8},{10,9},{11,1... | collective-permute-start | bytes 196616 | tf_op jit(solution)/shard_map/ppermute | solution.py:24
  74.2 22.0 %copy-start = (f32[2,10,32,128]{3,2,1,0:T(8,128)}, f32[2,10,32,128]{3,2,1,0:T(8,128)S(1)}, u32[]{:S(2)}) copy-start(f32[2,10,32,128]{3,2,1,0:T(8,128)S(1)} %fusion.25) | copy-start | bytes 983044
  77.3 18.9 %collective-permute-start.8 = (f32[2,2,32,128]{3,2,1,0:T(8,128)}, f32[2,2,32,128]{3,2,1,0:T(8,128)S(1)}, u32[]{:S(2)}, u32[]{:S(2)}) collective-permute-start(f32[2,2,32,128]{3,2,1,0:T(8,128)} %get-tuple-element.25), channel_id=1, source_target_pairs={{0,1},{1,2},{2,3},{3,4},{4,5},{5,6},{6,7},{7,8},{8,9},{9,10},{10,1... | collective-permute-start | bytes 196616 | tf_op jit(solution)/shard_map/ppermute | solution.py:22
  79.3 16.9 %collective-permute-start.9 = (f32[2,2,32,128]{3,2,1,0:T(8,128)}, f32[2,2,32,128]{3,2,1,0:T(8,128)}, u32[]{:S(2)}, u32[]{:S(2)}) collective-permute-start(f32[2,2,32,128]{3,2,1,0:T(8,128)} %get-tuple-element.26), channel_id=1, source_target_pairs={{1,0},{2,1},{3,2},{4,3},{5,4},{6,5},{7,6},{8,7},{9,8},{10,9},{11,1... | collective-permute-start | bytes 196616 | tf_op jit(solution)/shard_map/ppermute | solution.py:24
  96.2 0.7 copy-start.4
  96.2 0.7 copy-start.5
  99.4 1.1 copy-start.3
  102.0 32.8 %all-to-all-start = ((f32[2,2,32,1280]{3,1,0,2:T(2,128)}), f32[2,2,32,1280]{3,1,0,2:T(2,128)S(1)}, u32[]{:S(2)}, u32[]{:S(2)}) async-start(f32[2,2,32,1280]{3,1,0,2:T(2,128)} %copy.10), calls=%async_computation | async-start | bytes 1310720 | tf_op jit(solution)/shard_map/all_to_all | solution.py:65
